TPU v7x, 256 devices: a whole 4x4x8 slice. The times are simulated.
256 devices in a mesh: tile: 64 (over x, z, core), row: 4 (over y).
Axes of the slice: x: 4, y: 4, z: 8, core: 2. Of those that a mesh axis runs over, the one named last changes fastest.
Arguments:
- amplitudes: float32 [576, 64, 256], P('tile'), may hold values from -6 to 6
- integrals: float32 [4, 4096, 128, 256], P('row', 'tile'), may hold values from -0.0390625 to 0.0390625
- slot_ab: int32 [4, 4096], P('row', 'tile'), may hold values from 0 to 17
- slot_cd: int32 [4, 4096], P('row', 'tile'), may hold values from 0 to 575, as said below
- live_count: int32 [4, 64], P('row', 'tile'), may hold values from 1 to 64, as said below
- pair_list: int32 [64, 2], replicated, may hold values from 0 to 127, as said below
Outputs:
- symmetrized: float32 [64, 96, 96], P('tile', 'row')
Inputs may be any that keep to these rules, and one draw needn't show every extreme that they name: `slot_cd`: slot s of row index r belongs to tile index k = s // 64; its cd tile is held in amplitudes by tile index k - 1, k or k + 1, taken cyclically over the tile axis (cd tile c is held by tile index c // 9). `live_count`: slots at or after a device's count are unused. In every row index some device uses all 64 slots. `pair_list`: the rows are distinct pairs (i, j) with i != j, and for every row the reversed pair (j, i) is also a row.
All inputs are finite; a program needn't handle non-finite values.
Results may differ from a plain program's by a relative error of at most 0.0003.
Values sent between devices are 32-bit elements; how exact they have to be, the bound alone decides.
No kernel may reach another device: no remote copies, remote signals or barrier semaphores. Data moves between devices by JAX's collectives and lax.ppermute only.
A program may use at most 64 MiB of HBM per device.

v0:
```python
import jax
import jax.numpy as jnp
from jax import lax
from jax.sharding import PartitionSpec as P

TS = 16
ATS = 8
SLAB = 96


def padded(x, sides, width):
    for axis, dim in sides:
        size, length = (lax.axis_size(axis), x.shape[dim])
        up = [(i, (i + 1) % size) for i in range(size)]
        down = [(j, i) for i, j in up]
        last = lax.slice_in_dim(x, length - width, length, axis=dim)
        first = lax.slice_in_dim(x, 0, width, axis=dim)
        before = lax.ppermute(last, axis, up)
        after = lax.ppermute(first, axis, down)
        x = jnp.concatenate([before, x, after], axis=dim)
    return x


def find_mirror(pair_list):
    first_orb = pair_list[:, 0]
    second = pair_list[:, 1]
    matches = (first_orb[:, None] == second[None, :]) & (second[:, None] == first_orb[None, :])
    columns = jnp.arange(pair_list.shape[0], dtype=jnp.int32)
    return jnp.sum(jnp.where(matches, columns[None, :], 0), axis=1)


def to_grid(totals, a_tiles, b_tiles):
    pair_count = totals.shape[1]
    shaped = totals.reshape(a_tiles, b_tiles, pair_count, ATS, TS)
    return jnp.transpose(shaped, (2, 0, 3, 1, 4)).reshape(pair_count, a_tiles * ATS, b_tiles * TS)


def shards(amplitudes, integrals, slot_ab, slot_cd, live_count, pair_list):
    highest = lax.Precision.HIGHEST
    tile_size = lax.axis_size("tile")
    row_size = lax.axis_size("row")
    tile_index = lax.axis_index("tile")
    shard_tiles = amplitudes.shape[0]
    pair_count = amplitudes.shape[1]
    extended = padded(amplitudes, (("tile", 0),), shard_tiles)
    blocks_all = integrals[0]
    ab_local = slot_ab[0]
    cd_global = slot_cd[0]
    owner_tile = cd_global // shard_tiles
    offset = (owner_tile - tile_index + 1 + tile_size) % tile_size
    ext_index = offset * shard_tiles + cd_global % shard_tiles
    live_total = live_count[0, 0]
    a_tiles = SLAB // (row_size * ATS)
    b_tiles = SLAB // TS
    tiles_ab = a_tiles * b_tiles
    block_width = integrals.shape[2]
    group_size = 8

    def block_step(block_index, totals):
        first_slot = block_index * group_size
        picked = lax.dynamic_slice_in_dim(ext_index, first_slot, group_size)
        ab_tiles = lax.dynamic_slice_in_dim(ab_local, first_slot, group_size)
        blocks = lax.dynamic_slice_in_dim(blocks_all, first_slot, group_size, 0)
        live_mask = (first_slot + jnp.arange(group_size, dtype=jnp.int32) < live_total).astype(
            jnp.float32
        )
        amp_tiles = jnp.take(extended, picked, axis=0)
        products = jnp.einsum(
            "spw,sbw->spb", amp_tiles, blocks, precision=highest, preferred_element_type=jnp.float32
        )
        one_hot = (ab_tiles[:, None] == jnp.arange(tiles_ab, dtype=jnp.int32)[None, :]).astype(
            jnp.float32
        ) * live_mask[:, None]
        return totals + jnp.einsum(
            "se,spb->epb", one_hot, products, precision=highest, preferred_element_type=jnp.float32
        )

    turn_count = (live_total + group_size - 1) // group_size
    start_totals = jnp.zeros((tiles_ab, pair_count, block_width), jnp.float32)
    totals = lax.fori_loop(0, turn_count, block_step, start_totals)
    whole_term = to_grid(totals, a_tiles, b_tiles)
    mirror = find_mirror(pair_list)
    reduced = lax.psum_scatter(whole_term, "tile", scatter_dimension=0, tiled=True)
    exchanged = lax.all_to_all(reduced, "row", split_axis=2, concat_axis=1, tiled=True)
    turned = jnp.transpose(exchanged, (0, 2, 1))
    everyone = lax.all_gather(turned, "tile", axis=0, tiled=True)
    local_pairs = reduced.shape[0]
    wanted = lax.dynamic_slice_in_dim(mirror, tile_index * local_pairs, local_pairs)
    return reduced + jnp.take(everyone, wanted, axis=0)


def solution(mesh):
    return jax.shard_map(
        shards,
        mesh=mesh,
        in_specs=(
            P("tile", None, None),
            P("row", "tile", None, None),
            P("row", "tile"),
            P("row", "tile"),
            P("row", "tile"),
            P(),
        ),
        out_specs=P("tile", "row", None),
        check_vma=False,
    )
```

profile of v0, /device:TPU:1, one launch (start us, length us, event | category | flops | bytes accessed | tf_op | source)
XLA Modules:
  0.0 267.6 jit_solution(6142205821760800485)
XLA Ops:
  6.5 3.0 %collective-permute-start = (f32[9,64,256]{2,1,0:T(8,128)}, f32[9,64,256]{2,1,0:T(8,128)S(1)}, u32[]{:S(2)}, u32[]{:S(2)}) collective-permute-start(f32[9,64,256]{2,1,0:T(8,128)} %param.8), channel_id=1, source_target_pairs={{0,4},{4,8},{8,12},{12,16},{16,20},{20,24},{24,28},{28,32},{32,36}... | collective-permute-start | bytes 1769480 | tf_op jit(solution)/shard_map/ppermute | solution.py:18
  11.1 5.6 %collective-permute-done = f32[9,64,256]{2,1,0:T(8,128)S(1)} collective-permute-done((f32[9,64,256]{2,1,0:T(8,128)}, f32[9,64,256]{2,1,0:T(8,128)S(1)}, u32[]{:S(2)}, u32[]{:S(2)}) %collective-permute-start) | collective-permute-done | bytes 589856 | tf_op jit(solution)/shard_map/ppermute | solution.py:18
  16.7 2.7 collective-permute-done.1
  19.4 1.2 pad_maximum_fusion
  20.7 39.7 %while.11 = (s32[]{:T(128)}, f32[18,64,128]{2,0,1:T(8,128)S(1)}, s32[]{:T(128)}, s32[64]{0:T(128)S(1)}, s32[]{:T(128)}, /*index=5*/s32[64]{0:T(128)S(1)}, f32[27...) while((s32[]{:T(128)}, f32[18,64,128]{2,0,1:T(8,128)S(1)}, ...), condition=%wide.region_1.2_spmd, body=%wide.region_0.1_spmd.sunk | while | flops 215762288 | bytes 4329959 | solution.py:80
  22.0 2.5 fusion.28
  24.6 1.0 convolution_add_fusion.2
  25.6 0.7 compare_and_fusion.2
  27.0 2.5 fusion.28
  29.6 1.0 convolution_add_fusion.2
  31.9 2.5 fusion.28
  34.5 1.0 convolution_add_fusion.2
  35.6 0.7 compare_and_fusion.2
  36.9 2.5 fusion.28
  39.5 1.0 convolution_add_fusion.2
  41.9 2.5 fusion.28
  44.5 1.0 convolution_add_fusion.2
  45.5 0.7 compare_and_fusion.2
  46.8 2.5 fusion.28
  49.4 1.0 convolution_add_fusion.2
  50.5 0.7 compare_and_fusion.2
  51.8 2.5 fusion.28
  54.4 1.0 convolution_add_fusion.2
  56.8 2.5 fusion.28
  59.4 1.0 convolution_add_fusion.2
  60.9 1.2 copy.29
  62.2 128.7 %reduce-scatter.4.cloned.1.call-done = f32[1,24,96]{2,1,0:T(8,128)} async-done(((f32[64,24,96]{2,1,0:T(8,128)}), f32[1,24,96]{2,1,0:T(8,128)}) %reduce-scatter.4.cloned.1.call-update) | async-done | bytes 9232
  190.9 0.8 copy.30
  193.6 4.0 %all-to-all-start = ((f32[4,1,576]{2,1,0:T(1,128)}), f32[4,1,576]{2,1,0:T(1,128)S(1)}, u32[]{:S(2)}, u32[]{:S(2)}) async-start(f32[4,1,576]{2,1,0:T(1,128)} %reshape.79), calls=%async_computation | async-start | bytes 20480 | tf_op jit(solution)/shard_map/all_to_all | solution.py:84
  200.3 1.4 all-to-all-done
  202.8 56.7 %all_gather.3 = f32[64,24,96]{2,1,0:T(8,128)S(1)} all-gather(f32[1,24,96]{2,1,0:T(8,128)S(1)} %bitcast.48), channel_id=1, replica_groups=mesh['tile'=64,'row'=4] {'tile'}, dimensions={0}, use_global_device_ids=true | all-gather | bytes 599040 | tf_op jit(solution)/shard_map/all_gather | solution.py:86
  259.4 1.3 fusion.14
  (50 shorter events, 13.4 us)
Async XLA Ops:
  6.5 184.4 %reduce-scatter.4.cloned.1.call-start = ((), (), s32[]{:S(2)}) async-start(), calls=%async_computation.2 | async-start | bytes 798720
  6.5 10.2 %collective-permute-start = (f32[9,64,256]{2,1,0:T(8,128)}, f32[9,64,256]{2,1,0:T(8,128)S(1)}, u32[]{:S(2)}, u32[]{:S(2)}) collective-permute-start(f32[9,64,256]{2,1,0:T(8,128)} %param.8), channel_id=1, source_target_pairs={{0,4},{4,8},{8,12},{12,16},{16,20},{20,24},{24,28},{28,32},{32,36}... | collective-permute-start | bytes 1769480 | tf_op jit(solution)/shard_map/ppermute | solution.py:18
  9.6 9.8 %collective-permute-start.1 = (f32[9,64,256]{2,1,0:T(8,128)}, f32[9,64,256]{2,1,0:T(8,128)S(1)}, u32[]{:S(2)}, u32[]{:S(2)}) collective-permute-start(f32[9,64,256]{2,1,0:T(8,128)} %param.8), channel_id=1, source_target_pairs={{4,0},{8,4},{12,8},{16,12},{20,16},{24,20},{28,24},{32,28},{36,32}... | collective-permute-start | bytes 1769480 | tf_op jit(solution)/shard_map/ppermute | solution.py:19
  11.1 9.6 %copy-start.1 = (s32[1,64]{1,0:T(1,128)S(1)}, s32[1,64]{1,0:T(1,128)}, u32[]{:S(2)}) copy-start(s32[1,64]{1,0:T(1,128)} %param.10) | copy-start | bytes 772
  60.9 1.3 copy-start
  193.6 8.2 %all-to-all-start = ((f32[4,1,576]{2,1,0:T(1,128)}), f32[4,1,576]{2,1,0:T(1,128)S(1)}, u32[]{:S(2)}, u32[]{:S(2)}) async-start(f32[4,1,576]{2,1,0:T(1,128)} %reshape.79), calls=%async_computation | async-start | bytes 20480 | tf_op jit(solution)/shard_map/all_to_all | solution.py:84
Sparse Core Ops, SparseCore 0:
  62.3 128.5 reduce-scatter.3
where the time goes:
time: 268 us
  waiting for transfers between devices  138 us (51%)
  blocking collectives  56.7 us (21%)
  matrix products  28.3 us (11%)
  between operations  16.1 us (6%)
  other arithmetic  10.5 us (4%)
  local copies, waits for them, and re-layouts  10.1 us (4%)
  starting transfers between devices  7.18 us (3%)
    unnamed x2, waiting for transfers between devices  129 us
    all_gather x1, blocking collectives, shards(): everyone = lax.all_gather(turned, 'tile', axis=0, tiled=True)  56.7 us
    dot_general x8, matrix products, block_step(): jnp.einsum('spw,sbw->spb', amp_tiles, blocks, precision=highest, preferre...  20.3 us
    dot_general x8, matrix products, block_step(): jnp.einsum('se,spb->epb', one_hot, products, precision=highest, preferred...  8.01 us
    and x8, other arithmetic, block_step(): amp_tiles = jnp.take(extended, picked, axis=0)  5.82 us
    ppermute x1, waiting for transfers between devices, padded(): before = lax.ppermute(last, axis, up)  5.59 us
  transfers between devices with their start and end apart: 4, of which 4 were waited for; matrix products, arithmetic and copies ran while one was open for 1% of the time, Pallas kernels for 0%

commit v1 on v0

--- a/solution.py
+++ b/solution.py
@@ -83,7 +83,9 @@
     reduced = lax.psum_scatter(whole_term, "tile", scatter_dimension=0, tiled=True)
     exchanged = lax.all_to_all(reduced, "row", split_axis=2, concat_axis=1, tiled=True)
     turned = jnp.transpose(exchanged, (0, 2, 1))
-    everyone = lax.all_gather(turned, "tile", axis=0, tiled=True)
+    everyone = jnp.concatenate(
+        lax.all_to_all(jnp.stack([turned] * lax.axis_size("tile")), "tile", 0, 0), axis=0
+    )
     local_pairs = reduced.shape[0]
     wanted = lax.dynamic_slice_in_dim(mirror, tile_index * local_pairs, local_pairs)
     return reduced + jnp.take(everyone, wanted, axis=0)

time: 268 us -> 249 us (0.929)
  blocking collectives: 56.7 us -> 7.96 us
  waiting for transfers between devices: 138 us -> 157 us
  starting transfers between devices: 7.18 us -> 17.8 us
    all_gather x1 -> x0, blocking collectives: 56.7 us -> none  [shards(): everyone = lax.all_gather(turned, 'tile', axis=0, tiled=True)]
    all_to_all x1, waiting for transfers between devices: 1.44 us -> 20.2 us  [shards(): lax.all_to_all(jnp.stack([turned] * lax.axis_size('tile')), 'tile', 0, 0)]
    all_to_all x1, starting transfers between devices: 3.97 us -> 14.6 us  [shards(): lax.all_to_all(jnp.stack([turned] * lax.axis_size('tile')), 'tile', 0, 0)]
    all_to_all x0 -> x1, blocking collectives: none -> 7.96 us  [shards(): lax.all_to_all(reduced, 'row', split_axis=2, concat_axis=1, tiled=True)]
where the time goes in v1:
time: 249 us; the launch traced here: 248 us
  waiting for transfers between devices  157 us (63%)
  matrix products  28.3 us (11%)
  starting transfers between devices  17.8 us (7%)
  between operations  16.1 us (6%)
  local copies, waits for them, and re-layouts  10.5 us (4%)
  other arithmetic  9.99 us (4%)
  blocking collectives  7.96 us (3%)
    unnamed x2, waiting for transfers between devices  129 us
    dot_general x8, matrix products, block_step(): jnp.einsum('spw,sbw->spb', amp_tiles, blocks, precision=highest, preferre...  20.3 us
    all_to_all x1, waiting for transfers between devices, shards(): lax.all_to_all(jnp.stack([turned] * lax.axis_size('tile')), 'tile', 0, 0)  20.2 us
    all_to_all x1, starting transfers between devices, shards(): lax.all_to_all(jnp.stack([turned] * lax.axis_size('tile')), 'tile', 0, 0)  14.6 us
    dot_general x8, matrix products, block_step(): jnp.einsum('se,spb->epb', one_hot, products, precision=highest, preferred...  8.01 us
    all_to_all x1, blocking collectives, shards(): lax.all_to_all(reduced, 'row', split_axis=2, concat_axis=1, tiled=True)  7.96 us
    and x8, other arithmetic, block_step(): amp_tiles = jnp.take(extended, picked, axis=0)  5.82 us
    ppermute x1, waiting for transfers between devices, padded(): before = lax.ppermute(last, axis, up)  5.59 us
  transfers between devices with their start and end apart: 4, of which 4 were waited for; matrix products, arithmetic and copies ran while one was open for 1% of the time, Pallas kernels for 0%

profile of v1, /device:TPU:1, one launch (start us, length us, event | category | flops | bytes accessed | tf_op | source)
XLA Modules:
  0.0 248.1 jit_solution(10191683840620149851)
XLA Ops:
  6.5 3.0 %collective-permute-start = (f32[9,64,256]{2,1,0:T(8,128)}, f32[9,64,256]{2,1,0:T(8,128)S(1)}, u32[]{:S(2)}, u32[]{:S(2)}) collective-permute-start(f32[9,64,256]{2,1,0:T(8,128)} %param.8), channel_id=1, source_target_pairs={{0,4},{4,8},{8,12},{12,16},{16,20},{20,24},{24,28},{28,32},{32,36}... | collective-permute-start | bytes 1769480 | tf_op jit(solution)/shard_map/ppermute | solution.py:18
  11.1 5.6 %collective-permute-done = f32[9,64,256]{2,1,0:T(8,128)S(1)} collective-permute-done((f32[9,64,256]{2,1,0:T(8,128)}, f32[9,64,256]{2,1,0:T(8,128)S(1)}, u32[]{:S(2)}, u32[]{:S(2)}) %collective-permute-start) | collective-permute-done | bytes 589856 | tf_op jit(solution)/shard_map/ppermute | solution.py:18
  16.7 2.7 %collective-permute-done.1 = f32[9,64,256]{2,1,0:T(8,128)S(1)} collective-permute-done((f32[9,64,256]{2,1,0:T(8,128)}, f32[9,64,256]{2,1,0:T(8,128)S(1)}, u32[]{:S(2)}, u32[]{:S(2)}) %collective-permute-start.1) | collective-permute-done | bytes 589856 | tf_op jit(solution)/shard_map/ppermute | solution.py:19
  19.4 1.2 pad_maximum_fusion
  20.7 39.7 %while.11 = (s32[]{:T(128)}, f32[18,64,128]{2,0,1:T(8,128)S(1)}, s32[]{:T(128)}, s32[64]{0:T(128)S(1)}, s32[]{:T(128)}, /*index=5*/s32[64]{0:T(128)S(1)}, f32[27...) while((s32[]{:T(128)}, f32[18,64,128]{2,0,1:T(8,128)S(1)}, ...), condition=%wide.region_1.2_spmd, body=%wide.region_0.1_spmd.sunk | while | flops 215762288 | bytes 4329959 | solution.py:80
  22.0 2.5 %fusion.27 = f32[8,64,128]{2,1,0:T(8,128)S(1)} fusion(f32[64,128,256]{2,1,0:T(8,128)} %get-tuple-element.168, s32[]{:T(128)S(6)} %select_n.87, f32[8,64,256]{2,1,0:T(8,128)S(1)} %gather_fusion, pred[8]{0:T(512)(128)(4,1)S(1)} %get-tuple-element.135), kind=kOutput, calls=%fused_computation.2.clone.1 | convolution fusion | flops 201457664 | bytes 1835020 | tf_op jit(solution)/shard_map/while/body/spw,sbw->spb/dot_general | solution.py:68
  24.6 1.0 convolution_add_fusion.2
  25.6 0.7 compare_and_fusion.2
  27.0 2.5 %fusion.27 = f32[8,64,128]{2,1,0:T(8,128)S(1)} fusion(f32[64,128,256]{2,1,0:T(8,128)} %get-tuple-element.168, s32[]{:T(128)S(6)} %select_n.87, f32[8,64,256]{2,1,0:T(8,128)S(1)} %gather_fusion, pred[8]{0:T(512)(128)(4,1)S(1)} %get-tuple-element.135), kind=kOutput, calls=%fused_computation.2.clone.1 | convolution fusion | flops 201457664 | bytes 1835020 | tf_op jit(solution)/shard_map/while/body/spw,sbw->spb/dot_general | solution.py:68
  29.6 1.0 convolution_add_fusion.2
  31.9 2.5 %fusion.27 = f32[8,64,128]{2,1,0:T(8,128)S(1)} fusion(f32[64,128,256]{2,1,0:T(8,128)} %get-tuple-element.168, s32[]{:T(128)S(6)} %select_n.87, f32[8,64,256]{2,1,0:T(8,128)S(1)} %gather_fusion, pred[8]{0:T(512)(128)(4,1)S(1)} %get-tuple-element.135), kind=kOutput, calls=%fused_computation.2.clone.1 | convolution fusion | flops 201457664 | bytes 1835020 | tf_op jit(solution)/shard_map/while/body/spw,sbw->spb/dot_general | solution.py:68
  34.5 1.0 convolution_add_fusion.2
  35.6 0.7 compare_and_fusion.2
  36.9 2.5 %fusion.27 = f32[8,64,128]{2,1,0:T(8,128)S(1)} fusion(f32[64,128,256]{2,1,0:T(8,128)} %get-tuple-element.168, s32[]{:T(128)S(6)} %select_n.87, f32[8,64,256]{2,1,0:T(8,128)S(1)} %gather_fusion, pred[8]{0:T(512)(128)(4,1)S(1)} %get-tuple-element.135), kind=kOutput, calls=%fused_computation.2.clone.1 | convolution fusion | flops 201457664 | bytes 1835020 | tf_op jit(solution)/shard_map/while/body/spw,sbw->spb/dot_general | solution.py:68
  39.5 1.0 convolution_add_fusion.2
  41.9 2.5 %fusion.27 = f32[8,64,128]{2,1,0:T(8,128)S(1)} fusion(f32[64,128,256]{2,1,0:T(8,128)} %get-tuple-element.168, s32[]{:T(128)S(6)} %select_n.87, f32[8,64,256]{2,1,0:T(8,128)S(1)} %gather_fusion, pred[8]{0:T(512)(128)(4,1)S(1)} %get-tuple-element.135), kind=kOutput, calls=%fused_computation.2.clone.1 | convolution fusion | flops 201457664 | bytes 1835020 | tf_op jit(solution)/shard_map/while/body/spw,sbw->spb/dot_general | solution.py:68
  44.5 1.0 convolution_add_fusion.2
  45.5 0.7 compare_and_fusion.2
  46.8 2.5 %fusion.27 = f32[8,64,128]{2,1,0:T(8,128)S(1)} fusion(f32[64,128,256]{2,1,0:T(8,128)} %get-tuple-element.168, s32[]{:T(128)S(6)} %select_n.87, f32[8,64,256]{2,1,0:T(8,128)S(1)} %gather_fusion, pred[8]{0:T(512)(128)(4,1)S(1)} %get-tuple-element.135), kind=kOutput, calls=%fused_computation.2.clone.1 | convolution fusion | flops 201457664 | bytes 1835020 | tf_op jit(solution)/shard_map/while/body/spw,sbw->spb/dot_general | solution.py:68
  49.4 1.0 convolution_add_fusion.2
  51.8 2.5 %fusion.27 = f32[8,64,128]{2,1,0:T(8,128)S(1)} fusion(f32[64,128,256]{2,1,0:T(8,128)} %get-tuple-element.168, s32[]{:T(128)S(6)} %select_n.87, f32[8,64,256]{2,1,0:T(8,128)S(1)} %gather_fusion, pred[8]{0:T(512)(128)(4,1)S(1)} %get-tuple-element.135), kind=kOutput, calls=%fused_computation.2.clone.1 | convolution fusion | flops 201457664 | bytes 1835020 | tf_op jit(solution)/shard_map/while/body/spw,sbw->spb/dot_general | solution.py:68
  54.4 1.0 convolution_add_fusion.2
  56.8 2.5 %fusion.27 = f32[8,64,128]{2,1,0:T(8,128)S(1)} fusion(f32[64,128,256]{2,1,0:T(8,128)} %get-tuple-element.168, s32[]{:T(128)S(6)} %select_n.87, f32[8,64,256]{2,1,0:T(8,128)S(1)} %gather_fusion, pred[8]{0:T(512)(128)(4,1)S(1)} %get-tuple-element.135), kind=kOutput, calls=%fused_computation.2.clone.1 | convolution fusion | flops 201457664 | bytes 1835020 | tf_op jit(solution)/shard_map/while/body/spw,sbw->spb/dot_general | solution.py:68
  59.4 1.0 convolution_add_fusion.2
  60.9 1.2 copy.34
  62.2 128.7 %reduce-scatter.4.cloned.1.call-done = f32[1,24,96]{2,1,0:T(8,128)} async-done(((f32[64,24,96]{2,1,0:T(8,128)}), f32[1,24,96]{2,1,0:T(8,128)}) %reduce-scatter.4.cloned.1.call-update) | async-done | bytes 9232
  190.9 0.9 copy.35
  192.3 0.8 reduce
  193.2 8.0 %all_to_all.23 = f32[4,1,576]{2,1,0:T(1,128)S(1)} all-to-all(f32[4,1,576]{2,1,0:T(1,128)S(1)} %reshape.90), channel_id=1, replica_groups=mesh['tile'=64,'row'=4] {'row'}, dimensions={0} | all-to-all | bytes 18432 | tf_op jit(solution)/shard_map/all_to_all | solution.py:84
  202.2 0.9 stack.2
  203.2 14.6 %all-to-all-start.1 = ((f32[64,1,24,96]{3,2,1,0:T(8,128)}), f32[64,1,24,96]{3,2,1,0:T(8,128)S(1)}, u32[]{:S(2)}, u32[]{:S(2)}) async-start(f32[64,1,24,96]{3,2,1,0:T(8,128)} %stack.2), calls=%async_computation.1 | async-start | bytes 1572864 | tf_op jit(solution)/shard_map/all_to_all | solution.py:87
  220.5 20.2 %all-to-all-done.1 = f32[64,1,24,96]{3,2,1,0:T(8,128)S(1)} async-done(((f32[64,1,24,96]{3,2,1,0:T(8,128)}), f32[64,1,24,96]{3,2,1,0:T(8,128)S(1)}, u32[]{:S(2)}, u32[]{:S(2)}) %all-to-all-start.1) | async-done | bytes 589856 | tf_op jit(solution)/shard_map/all_to_all | solution.py:87
  (53 shorter events, 13.5 us)
Async XLA Ops:
  6.5 184.4 %reduce-scatter.4.cloned.1.call-start = ((), (), s32[]{:S(2)}) async-start(), calls=%async_computation.3 | async-start | bytes 798720
  6.5 10.2 %collective-permute-start = (f32[9,64,256]{2,1,0:T(8,128)}, f32[9,64,256]{2,1,0:T(8,128)S(1)}, u32[]{:S(2)}, u32[]{:S(2)}) collective-permute-start(f32[9,64,256]{2,1,0:T(8,128)} %param.8), channel_id=1, source_target_pairs={{0,4},{4,8},{8,12},{12,16},{16,20},{20,24},{24,28},{28,32},{32,36}... | collective-permute-start | bytes 1769480 | tf_op jit(solution)/shard_map/ppermute | solution.py:18
  9.6 9.8 %collective-permute-start.1 = (f32[9,64,256]{2,1,0:T(8,128)}, f32[9,64,256]{2,1,0:T(8,128)S(1)}, u32[]{:S(2)}, u32[]{:S(2)}) collective-permute-start(f32[9,64,256]{2,1,0:T(8,128)} %param.8), channel_id=1, source_target_pairs={{4,0},{8,4},{12,8},{16,12},{20,16},{24,20},{28,24},{32,28},{36,32}... | collective-permute-start | bytes 1769480 | tf_op jit(solution)/shard_map/ppermute | solution.py:19
  11.1 9.6 %copy-start.2 = (s32[1,64]{1,0:T(1,128)S(1)}, s32[1,64]{1,0:T(1,128)}, u32[]{:S(2)}) copy-start(s32[1,64]{1,0:T(1,128)} %param.10) | copy-start | bytes 772
  62.2 155.6 %copy-start.1 = (s32[64,2]{0,1:T(2,128)S(1)}, s32[64,2]{0,1:T(2,128)}, u32[]{:S(2)}) copy-start(s32[64,2]{0,1:T(2,128)} %param.13) | copy-start | bytes 1540
  190.9 49.8 %copy-start = (f32[1,24,96]{2,1,0:T(8,128)S(1)}, f32[1,24,96]{2,1,0:T(8,128)}, u32[]{:S(2)}) copy-start(f32[1,24,96]{2,1,0:T(8,128)} %reduce-scatter.4.cloned.1.call-done) | copy-start | bytes 27652
  203.2 37.5 %all-to-all-start.1 = ((f32[64,1,24,96]{3,2,1,0:T(8,128)}), f32[64,1,24,96]{3,2,1,0:T(8,128)S(1)}, u32[]{:S(2)}, u32[]{:S(2)}) async-start(f32[64,1,24,96]{3,2,1,0:T(8,128)} %stack.2), calls=%async_computation.1 | async-start | bytes 1572864 | tf_op jit(solution)/shard_map/all_to_all | solution.py:87
Sparse Core Ops, SparseCore 0:
  62.3 128.5 reduce-scatter.3
